TPU v7x, 32 devices: a whole 2x2x4 slice. The times are simulated.
32 devices in a mesh: row: 4 (over y, x), col: 8 (over z, core).
Axes of the slice: x: 2, y: 2, z: 4, core: 2. Of those that a mesh axis runs over, the one named last changes fastest.
Arguments:
- covariance: float32 [20, 4, 10, 8, 256, 256], P(None, 'row', None, 'col'), may hold values from -0.006 to 2.4, as said below
- telemetry: bfloat16 [1536, 10, 8, 256], P('row', None, 'col'), may hold values from -6 to 6
- active: int32 [8, 1280], replicated, may hold values 0 or 1
- panel: int32 [1], replicated, may hold values from 0 to 75
Outputs:
- factored: float32 [20, 4, 10, 8, 256, 256], P(None, 'row', None, 'col')
Inputs may be any that keep to these rules, and one draw needn't show every extreme that they name: `covariance`: in every diagonal tile each diagonal entry exceeds the sum of magnitudes of the other entries of its row; entries off the matrix diagonal lie in -0.006 to 0.006.
All inputs are finite; a program needn't handle non-finite values.
Results may differ from a plain program's by a relative error of at most 0.0006.
Values may be sent and summed in bfloat16 or wider, within the bound.
No kernel may reach another device: no remote copies, remote signals or barrier semaphores. Data moves between devices by JAX's collectives and lax.ppermute only.
A program may use at most 384 MiB of HBM per device.

v0:
```python
import jax
import jax.numpy as jnp
from jax import lax
from jax.sharding import PartitionSpec as P

FORGET = 0.9


def from_root(block, axis, holder):
    block = jnp.where(lax.axis_index(axis) == holder, block, jnp.zeros_like(block))
    return lax.psum(block, axis)


def body(covariance, telemetry, active, panel):
    n_row = lax.axis_size("row")
    n_col = lax.axis_size("col")
    row_index = lax.axis_index("row")
    col_index = lax.axis_index("col")
    blocks_a = covariance.shape[0]
    blocks_b = covariance.shape[2]
    width = covariance.shape[4]
    ratio = n_col // n_row
    samples = telemetry.shape[0] * n_row
    tiles = blocks_b * n_col
    earlier = covariance[:, 0, :, 0]
    local = telemetry[:, :, 0, :]
    mask_full = jnp.concatenate([active, active], axis=1).reshape(tiles, width).astype(jnp.bfloat16)
    col_mask = lax.dynamic_index_in_dim(
        mask_full.reshape(blocks_b, n_col, width), col_index, 1, keepdims=False
    )
    row_mask = lax.dynamic_index_in_dim(
        mask_full.reshape(blocks_a, n_row, width), row_index, 1, keepdims=False
    )
    column_data = lax.all_gather(local, "row", axis=0, tiled=True)
    slabs = []
    for offset in range(ratio):
        slabs.append(from_root(column_data, "col", row_index + offset * n_row))
    row_data = jnp.stack(slabs, axis=2).reshape(samples, blocks_a, width)
    column_data = column_data * col_mask[None]
    row_data = row_data * row_mask[None]
    row_tiles = jnp.arange(blocks_a, dtype=jnp.int32) * n_row + row_index
    col_tiles = jnp.arange(blocks_b, dtype=jnp.int32) * n_col + col_index
    lower = row_tiles[:, None] >= col_tiles[None, :]
    gram = jnp.einsum("sat,sbu->abtu", row_data, column_data, preferred_element_type=jnp.float32)
    fresh = jnp.where(lower[:, :, None, None], FORGET * earlier + gram / samples, earlier)
    panel_at = panel[0]
    owner_row = panel_at % n_row
    owner_col = panel_at % n_col
    diag_tile = lax.dynamic_slice(
        fresh, (panel_at // n_row, panel_at // n_col, 0, 0), (1, 1, width, width)
    )[0, 0]
    factor = jnp.linalg.cholesky(diag_tile)
    inverse = lax.linalg.triangular_solve(
        factor, jnp.eye(width, dtype=jnp.float32), left_side=True, lower=True
    )
    inverse = from_root(inverse, "row", owner_row)
    column_part = lax.dynamic_index_in_dim(fresh, panel_at // n_col, 1, keepdims=False)
    solved = jnp.einsum(
        "atu,vu->atv",
        column_part,
        inverse,
        precision=lax.Precision.HIGHEST,
        preferred_element_type=jnp.float32,
    )
    solved = jnp.where((row_tiles > panel_at)[:, None, None], solved, jnp.zeros_like(solved))
    panel_rows = from_root(solved.astype(jnp.bfloat16), "col", owner_col).astype(solved.dtype)
    pick = col_index // n_row
    chosen = lax.dynamic_index_in_dim(
        panel_rows.reshape(blocks_b, ratio, width, width), pick, 1, keepdims=False
    )
    panel_cols = from_root(chosen.astype(jnp.bfloat16), "row", col_index % n_row).astype(
        chosen.dtype
    )
    trailing = lower & (col_tiles[None, :] > panel_at)
    update = jnp.einsum(
        "atv,buv->abtu",
        panel_rows,
        panel_cols,
        precision=lax.Precision.HIGHEST,
        preferred_element_type=jnp.float32,
    )
    result = jnp.where(trailing[:, :, None, None], fresh - update, fresh)
    on_column = (col_tiles == panel_at)[None, :] & (row_tiles > panel_at)[:, None]
    result = jnp.where(on_column[:, :, None, None], panel_rows[:, None], result)
    on_diagonal = (col_tiles == panel_at)[None, :] & (row_tiles == panel_at)[:, None]
    result = jnp.where(on_diagonal[:, :, None, None], factor[None, None], result)
    return result[:, None, :, None]


def solution(mesh):
    in_specs = (P(None, "row", None, "col", None, None), P("row", None, "col", None), P(), P())
    out_specs = P(None, "row", None, "col", None, None)
    return jax.shard_map(body, mesh=mesh, in_specs=in_specs, out_specs=out_specs, check_vma=False)
```

profile of v0, /device:TPU:0, one launch (start us, length us, event | category | flops | bytes accessed | tf_op | source)
XLA Modules:
  0.0 831.1 jit_solution(5645800348601662963)
XLA Ops:
  6.5 0.7 all-gather.3.cloned.1.call-update
  7.3 87.7 %all-gather.3.cloned.1.call-done = bf16[1536,10,1,256]{3,0,1,2:T(8,128)(2,1)} async-done(((bf16[384,10,1,256]{3,0,1,2:T(8,128)(2,1)}), bf16[1536,10,1,256]{3,0,1,2:T(8,128)(2,1)}) %all-gather.3.cloned.1.call-update) | async-done | bytes 7864336 | tf_op jit(solution)/shard_map/all_gather | solution.py:34
  95.0 9.7 %fusion.6 = (bf16[1536,10,1,256]{3,0,1,2:T(8,128)(2,1)}, bf16[1536,10,1,256]{3,0,2,1:T(8,128)(2,1)}) fusion(bf16[1536,10,1,256]{3,0,1,2:T(8,128)(2,1)} %all-gather.3.cloned.1.call-done, pred[]{:T(512)S(6)} %eq.50, pred[]{:T(512)S(6)} %eq.51), kind=kLoop, calls=%fused_computation.16 | loop fusion | flops 7864320 | bytes 23592962 | tf_op jit(solution)/shard_map/stack | solution.py:38
  105.8 49.6 %copy.22 = f32[20,1,10,1,256,256]{4,5,0,2,3,1:T(8,128)} copy(f32[20,1,10,1,256,256]{5,4,3,2,1,0:T(8,128)} %param.4) | data formatting | bytes 104857600 | tf_op args[0]
  155.6 263.2 %all-reduce.13.cloned.1.call-done = (bf16[1536,10,1,256]{3,0,2,1:T(8,128)(2,1)}, bf16[1536,10,1,256]{3,0,1,2:T(8,128)(2,1)}) async-done(((bf16[1536,10,1,256]{3,0,2,1:T(8,128)(2,1)}, bf16[1536,10,1,256]{3,0,1,2:T(8,128)(2,1)}), (bf16[1536,10,1,256]{3,0,2,1:T(8,128)(2,1)}, bf16[1536,10,1,256]{3,0,1,2:T(8,128)(2,1)})) %all-reduce.13.cloned.1.call-update) | async-done | bytes 15728656 | tf_op jit(solution)/shard_map/psum | solution.py:11
  418.8 7.8 pad_maximum_fusion
  426.6 6.5 bitcast_multiply_fusion.1
  433.1 56.1 %fusion.3 = f32[20,10,256,256]{2,3,0,1:T(8,128)} fusion(f32[20,1,10,1,256,256]{4,5,0,2,3,1:T(8,128)} %copy.22, pred[20,10]{0,1:T(8,128)(4,1)S(1)} %get-tuple-element.34, bf16[1536,20,256]{2,0,1:T(8,128)(2,1)} %bitcast_multiply_fusion.1, bf16[1536,10,1,256]{3,0,1,2:T(8,128)(2,1)} %all-gather.3.cloned.1.call-done, bf16[10,256]{1,0:T(8,128)(2,1)S(1)} %bitcast.126), kind=kOutput, calls=%fused_computation.7 | convolution fusion | flops 40333475840 | bytes 128455880 | tf_op jit(solution)/shard_map/sat,sbu->abtu/dot_general | solution.py:44
  489.2 1.0 dynamic-slice_bitcast_fusion
  490.3 1.0 fusion.19
  491.3 11.7 %cholesky.50 = f32[128,128]{1,0:T(8,128)S(1)} custom-call(f32[128,128]{1,0:T(8,128)S(1)} %cholesky.118), custom_call_target="Cholesky" | custom-call | tf_op jit(solution)/shard_map/jit(cholesky)/cholesky | solution.py:52
  503.1 9.8 %custom-call.14 = f32[1,128,128]{1,2,0:T(8,128)S(1)} custom-call(f32[1,128,128]{2,1,0:T(8,128)S(1)} %get-tuple-element.32), custom_call_target="InvertDiagBlocksLowerTriangular" | custom-call | tf_op jit(solution)/shard_map/jit(cholesky)/cholesky | solution.py:52
  513.1 0.3 convolution_subtract_fusion.1
  513.4 11.7 %cholesky.105 = f32[128,128]{1,0:T(8,128)S(1)} custom-call(f32[128,128]{1,0:T(8,128)S(1)} %convolution_subtract_fusion.1), custom_call_target="Cholesky" | custom-call | tf_op jit(solution)/shard_map/jit(cholesky)/cholesky | solution.py:52
  525.2 0.7 compare_reduce_fusion
  527.3 3.9 while.1
  527.3 0.6 fusion.39
  527.9 1.3 bitcast_dynamic-update-slice_fusion.2
  529.2 0.6 fusion.39
  529.8 1.3 bitcast_dynamic-update-slice_fusion.2
  531.2 19.9 %custom-call.15 = f32[2,128,128]{1,2,0:T(8,128)S(1)} custom-call(f32[2,128,128]{2,1,0:T(8,128)S(1)} %get-tuple-element.12), custom_call_target="InvertDiagBlocksLowerTriangular" | custom-call | tf_op jit(solution)/shard_map/triangular_solve | solution.py:53
  551.1 0.3 fusion.22
  551.6 0.3 fusion.25
  551.9 0.7 maximum_select_fusion
  552.8 43.4 %all-reduce.7.cloned.1.call-done = f32[256,256]{1,0:T(8,128)} async-done(((f32[256,256]{1,0:T(8,128)}), f32[256,256]{1,0:T(8,128)}) %all-reduce.7.cloned.1.call-update) | async-done | bytes 262160 | tf_op jit(solution)/shard_map/psum | solution.py:11
  596.1 12.9 %fusion.12 = bf16[20,256,256]{2,1,0:T(8,128)(2,1)} fusion(pred[20]{0:T(512)(128)(4,1)S(1)} %broadcast_compare_fusion.1, pred[]{:T(512)S(6)} %eq.52, f32[20,10,256,256]{2,3,0,1:T(8,128)} %fusion.3, s32[]{:T(128)S(6)} %select_n.120, f32[256,256]{1,0:T(8,128)} %all-reduce.7.cloned.1.call-done), kind=kOutput, calls=%fused_computation.23 | convolution fusion | flops 4030464000 | bytes 8126489 | tf_op jit(solution)/shard_map/atu,vu->atv/dot_general | solution.py:58
  609.1 69.2 %all-reduce.9.cloned.1.call-done = bf16[20,256,256]{2,1,0:T(8,128)(2,1)} async-done(((bf16[20,256,256]{2,1,0:T(8,128)(2,1)}), bf16[20,256,256]{2,1,0:T(8,128)(2,1)}) %all-reduce.9.cloned.1.call-update) | async-done | bytes 2621456 | tf_op jit(solution)/shard_map/psum | solution.py:11
  678.3 2.6 fusion.17
  681.2 5.1 copy.29
  686.4 50.4 %all-reduce.11.cloned.1.call-done = bf16[10,256,256]{2,1,0:T(8,128)(2,1)} async-done(((bf16[10,256,256]{2,1,0:T(8,128)(2,1)}), bf16[10,256,256]{2,1,0:T(8,128)(2,1)}) %all-reduce.11.cloned.1.call-update) | async-done | bytes 1310736 | tf_op jit(solution)/shard_map/psum | solution.py:11
  736.8 35.7 %fusion.2 = f32[20,1,10,1,256,256]{4,5,0,2,3,1:T(8,128)} fusion(f32[20,10,256,256]{2,3,0,1:T(8,128)} %fusion.3, f32[20,256,256]{1,2,0:T(8,128)} %copy.29, f32[256,256]{0,1:T(8,128)S(1)} %copy.27, pred[20,10]{0,1:T(8,128)(4,1)S(1)} %get-tuple-element.33, pred[20,10]{0,1:T(8,128)(4,1)S(1)} %get-tuple-element.36, pred[20,10]{0,1:T(8,128)(4,1)S(1)} %get-tuple-element.35, ...), kind=kOutput, calls=%fused_computation.5 | convolution fusion | flops 6763315200 | bytes 114295384 | tf_op jit(solution)/shard_map/atv,buv->abtu/dot_general | solution.py:75
  772.4 52.2 %copy.31 = f32[20,1,10,1,256,256]{5,4,3,2,1,0:T(8,128)} copy(f32[20,1,10,1,256,256]{4,5,0,2,3,1:T(8,128)} %fusion.2) | data formatting | bytes 104857600 | tf_op jit(solution)/shard_map/broadcast_in_dim | solution.py:87
  (43 shorter events, 1.6 us)
Async XLA Ops:
  6.5 88.5 %all-gather.3.cloned.1.call-start = ((), (), s32[]{:S(2)}) async-start(), calls=%async_computation.3 | async-start | bytes 9830400 | tf_op jit(solution)/shard_map/all_gather | solution.py:34
  7.3 411.6 %all-reduce.13.cloned.1.call-start = ((), (), s32[]{:S(2)}) async-start(), calls=%async_computation.4 | async-start | bytes 31457280 | tf_op jit(solution)/shard_map/psum | solution.py:11
  104.8 0.8 copy-start.1
  104.8 491.3 %all-reduce.7.cloned.1.call-start = ((), (), s32[]{:S(2)}) async-start(), calls=%async_computation | async-start | bytes 524288 | tf_op jit(solution)/shard_map/psum | solution.py:11
  552.7 125.7 %all-reduce.9.cloned.1.call-start = ((), (), s32[]{:S(2)}) async-start(), calls=%async_computation.1 | async-start | bytes 5242880 | tf_op jit(solution)/shard_map/psum | solution.py:11
  609.1 127.7 %all-reduce.11.cloned.1.call-start = ((), (), s32[]{:S(2)}) async-start(), calls=%async_computation.2 | async-start | bytes 2621440 | tf_op jit(solution)/shard_map/psum | solution.py:11
  678.3 58.4 %copy-start = (bf16[20,256,256]{2,1,0:T(8,128)(2,1)S(1)}, bf16[20,256,256]{2,1,0:T(8,128)(2,1)}, u32[]{:S(2)}) copy-start(bf16[20,256,256]{2,1,0:T(8,128)(2,1)} %all-reduce.9.cloned.1.call-done) | copy-start | bytes 7864324
Sparse Core Ops, SparseCore 0:
  9.2 85.8 all-gather.2
  104.9 313.8 all-reduce.12
  552.8 43.3 all-reduce.6
  609.2 69.1 all-reduce.8
  681.3 55.4 all-reduce.10
where the time goes:
time: 833 us; the launch traced here: 831 us
  waiting for transfers between devices  515 us (62%)
  local copies, waits for them, and re-layouts  112 us (13%)
  matrix products  106 us (13%)
  other arithmetic  82.5 us (10%)
  between operations  15.4 us (2%)
    psum x4, waiting for transfers between devices, from_root(): return lax.psum(block, axis)  426 us
    all_gather x1, waiting for transfers between devices, body(): column_data = lax.all_gather(local, 'row', axis=0, tiled=True)  87.7 us
    dot_general x1, matrix products, body(): jnp.einsum('sat,sbu->abtu', row_data, column_data, preferred_element_type...  56.1 us
    broadcast_in_dim x1, local copies, waits for them, and re-layouts, body(): return result[:, None, :, None]  52.2 us
    unnamed x7, local copies, waits for them, and re-layouts  49.6 us
    dot_general x1, matrix products, body(): jnp.einsum('atv,buv->abtu', panel_rows, panel_cols, precision=lax.Precisi...  35.7 us
    another operation x6, other arithmetic, body(): factor = jnp.linalg.cholesky(diag_tile)  34 us
    another operation x3, other arithmetic, body(): lax.linalg.triangular_solve(factor, jnp.eye(width, dtype=jnp.float32), le...  19.9 us
  transfers between devices with their start and end apart: 5, of which 5 were waited for; matrix products, arithmetic and copies ran while one was open for 7% of the time, Pallas kernels for 0%

commit v1 on v0

v1 whole, which is shorter than its diff:
```python
import functools

import jax
import jax.numpy as jnp
from jax import lax
from jax.experimental import pallas as pl
from jax.experimental.pallas import tpu as pltpu
from jax.sharding import PartitionSpec as P

FORGET = 0.9


def from_root(block, axis, holder):
    block = jnp.where(lax.axis_index(axis) == holder, block, jnp.zeros_like(block))
    return lax.psum(block, axis)


def refresh_kernel(ids_ref, rowt_ref, col_ref, c_ref, o_ref, *, n_row, n_col, width, samples):
    a = pl.program_id(0)
    b = pl.program_id(1)
    i = a * n_row + ids_ref[0]
    j = b * n_col + ids_ref[1]
    prior = c_ref[0, 0, 0, 0]

    @pl.when(i >= j)
    def _():
        start = pl.multiple_of(b * width, width)
        cols = col_ref[:, pl.ds(start, width)]
        gram = jnp.dot(rowt_ref[0], cols, preferred_element_type=jnp.float32)
        o_ref[0, 0, 0, 0] = FORGET * prior + gram / samples

    @pl.when(i < j)
    def _():
        o_ref[0, 0, 0, 0] = prior


def update_kernel(ids_ref, r_ref, prow_ref, pcol_ref, fac_ref, o_ref, *, n_row, n_col):
    a = pl.program_id(0)
    b = pl.program_id(1)
    i = a * n_row + ids_ref[0]
    j = b * n_col + ids_ref[1]
    k = ids_ref[2]
    trailing = (i >= j) & (j > k)
    on_column = (j == k) & (i > k)
    on_diagonal = (j == k) & (i == k)
    keep = jnp.logical_not(trailing | on_column | on_diagonal)

    @pl.when(trailing)
    def _():
        upd = lax.dot_general(
            prow_ref[0], pcol_ref[0], (((1,), (1,)), ((), ())), preferred_element_type=jnp.float32
        )
        o_ref[0, 0, 0, 0] = r_ref[0, 0, 0, 0] - upd

    @pl.when(on_column)
    def _():
        o_ref[0, 0, 0, 0] = prow_ref[0].astype(jnp.float32)

    @pl.when(on_diagonal)
    def _():
        o_ref[0, 0, 0, 0] = fac_ref[...]

    @pl.when(keep)
    def _():
        o_ref[0, 0, 0, 0] = r_ref[0, 0, 0, 0]


def body(covariance, telemetry, active, panel, *, n_row, n_col):
    row_index = lax.axis_index("row")
    col_index = lax.axis_index("col")
    blocks_a = covariance.shape[0]
    blocks_b = covariance.shape[2]
    width = covariance.shape[4]
    ratio = n_col // n_row
    s_local = telemetry.shape[0]
    samples = s_local * n_row
    tiles = blocks_b * n_col
    local = telemetry[:, :, 0, :]
    mask_full = jnp.concatenate([active, active], axis=1).reshape(tiles, width).astype(jnp.bfloat16)
    col_mask = lax.dynamic_index_in_dim(
        mask_full.reshape(blocks_b, n_col, width), col_index, 1, keepdims=False
    )
    local = local * col_mask[None]

    column_data = lax.all_gather(local, "row", axis=0, tiled=True)
    perm = []
    for src_r in range(n_row):
        for src_c in range(n_col):
            dst_r = src_c % n_row
            dst_c = ratio * src_r + src_c // n_row
            perm.append((src_r * n_col + src_c, dst_r * n_col + dst_c))
    piece = lax.ppermute(local, ("row", "col"), perm)
    row_g = lax.all_gather(piece, "col", axis=0, tiled=False)
    row_g = row_g.reshape(n_row, ratio, s_local, blocks_b, width)
    row_t = jnp.transpose(row_g, (3, 1, 4, 0, 2)).reshape(blocks_a, width, samples)
    col_flat = column_data.reshape(samples, blocks_b * width)

    panel_at = panel[0]
    ids = jnp.stack([row_index, col_index, panel_at]).astype(jnp.int32)

    refreshed = pl.pallas_call(
        functools.partial(refresh_kernel, n_row=n_row, n_col=n_col, width=width, samples=samples),
        out_shape=jax.ShapeDtypeStruct(covariance.shape, jnp.float32),
        grid_spec=pltpu.PrefetchScalarGridSpec(
            num_scalar_prefetch=1,
            grid=(blocks_a, blocks_b),
            in_specs=[
                pl.BlockSpec((1, width, samples), lambda a, b, ids: (a, 0, 0)),
                pl.BlockSpec((samples, blocks_b * width), lambda a, b, ids: (0, 0)),
                pl.BlockSpec((1, 1, 1, 1, width, width), lambda a, b, ids: (a, 0, b, 0, 0, 0)),
            ],
            out_specs=pl.BlockSpec((1, 1, 1, 1, width, width), lambda a, b, ids: (a, 0, b, 0, 0, 0)),
        ),
        compiler_params=pltpu.CompilerParams(vmem_limit_bytes=48 * 1024 * 1024),
    )(ids, row_t, col_flat, covariance)

    fresh = refreshed[:, 0, :, 0]
    owner_row = panel_at % n_row
    owner_col = panel_at % n_col
    row_tiles = jnp.arange(blocks_a, dtype=jnp.int32) * n_row + row_index
    diag_tile = lax.dynamic_slice(
        fresh, (panel_at // n_row, panel_at // n_col, 0, 0), (1, 1, width, width)
    )[0, 0]
    factor = jnp.linalg.cholesky(diag_tile)
    inverse = lax.linalg.triangular_solve(
        factor, jnp.eye(width, dtype=jnp.float32), left_side=True, lower=True
    )
    inverse = from_root(inverse, "row", owner_row)
    column_part = lax.dynamic_index_in_dim(fresh, panel_at // n_col, 1, keepdims=False)
    solved = jnp.einsum(
        "atu,vu->atv",
        column_part,
        inverse,
        precision=lax.Precision.HIGHEST,
        preferred_element_type=jnp.float32,
    )
    solved = jnp.where((row_tiles > panel_at)[:, None, None], solved, jnp.zeros_like(solved))
    panel_rows = from_root(solved.astype(jnp.bfloat16), "col", owner_col)
    pick = col_index // n_row
    chosen = lax.dynamic_index_in_dim(
        panel_rows.reshape(blocks_b, ratio, width, width), pick, 1, keepdims=False
    )
    panel_cols = from_root(chosen, "row", col_index % n_row)

    result = pl.pallas_call(
        functools.partial(update_kernel, n_row=n_row, n_col=n_col),
        out_shape=jax.ShapeDtypeStruct(covariance.shape, jnp.float32),
        grid_spec=pltpu.PrefetchScalarGridSpec(
            num_scalar_prefetch=1,
            grid=(blocks_a, blocks_b),
            in_specs=[
                pl.BlockSpec((1, 1, 1, 1, width, width), lambda a, b, ids: (a, 0, b, 0, 0, 0)),
                pl.BlockSpec((1, width, width), lambda a, b, ids: (a, 0, 0)),
                pl.BlockSpec((1, width, width), lambda a, b, ids: (b, 0, 0)),
                pl.BlockSpec((width, width), lambda a, b, ids: (0, 0)),
            ],
            out_specs=pl.BlockSpec((1, 1, 1, 1, width, width), lambda a, b, ids: (a, 0, b, 0, 0, 0)),
        ),
        input_output_aliases={1: 0},
    )(ids, refreshed, panel_rows, panel_cols, factor)
    return result


def solution(mesh):
    n_row = mesh.shape["row"]
    n_col = mesh.shape["col"]
    in_specs = (P(None, "row", None, "col", None, None), P("row", None, "col", None), P(), P())
    out_specs = P(None, "row", None, "col", None, None)
    return jax.shard_map(
        functools.partial(body, n_row=n_row, n_col=n_col),
        mesh=mesh,
        in_specs=in_specs,
        out_specs=out_specs,
        check_vma=False,
    )
```

time: 833 us -> 917 us (1.10)
  Pallas kernels: 0 us -> 266 us
  matrix products: 106 us -> 9.61 us
  waiting for transfers between devices: 515 us -> 460 us
  other arithmetic: 82.5 us -> 61.4 us
  local copies, waits for them, and re-layouts: 112 us -> 93.3 us
    pallas_call x0 -> x2, Pallas kernels: none -> 266 us  [the longest x1 143 us: body(): pl.pallas_call(functools.partial(refresh_kernel, n_row=n_row, n_col=n_col...]
    psum x4 -> x3, waiting for transfers between devices: 426 us -> 166 us  [from_root(): return lax.psum(block, axis)]
    all_gather x0 -> x1, waiting for transfers between devices: none -> 135 us  [body(): row_g = lax.all_gather(piece, 'col', axis=0, tiled=False)]
    dot_general x2 -> x0, matrix products: 91.8 us -> none  [the longest x1 56.1 us: body(): jnp.einsum('sat,sbu->abtu', row_data, column_data, preferred_element_type...]
    reshape x0 -> x4, local copies, waits for them, and re-layouts: none -> 84.1 us  [the longest x2 47.8 us: body(): row_g = row_g.reshape(n_row, ratio, s_local, blocks_b, width)]
    all_gather x1, waiting for transfers between devices: 87.7 us -> 158 us  [body(): column_data = lax.all_gather(local, 'row', axis=0, tiled=True)]
    broadcast_in_dim x1 -> x0, local copies, waits for them, and re-layouts: 52.2 us -> none  [body(): return result[:, None, :, None]]
    unnamed x7 -> x6, local copies, waits for them, and re-layouts: 49.6 us -> 4.23 us
  transfers between devices with their start and end apart: 5 -> 6, of which waited for: 5 -> 5; matrix products, arithmetic and copies ran while one was open for 7% -> 1% of each run, Pallas kernels for 0% -> 0%
where the time goes in v1:
time: 917 us; the launch traced here: 908 us
  waiting for transfers between devices  460 us (50%)
  Pallas kernels  266 us (29%)
  local copies, waits for them, and re-layouts  93.3 us (10%)
  other arithmetic  61.4 us (7%)
  between operations  15.2 us (2%)
  matrix products  9.61 us (1%)
    psum x3, waiting for transfers between devices, from_root(): return lax.psum(block, axis)  166 us
    all_gather x1, waiting for transfers between devices, body(): column_data = lax.all_gather(local, 'row', axis=0, tiled=True)  158 us
    pallas_call x1, Pallas kernels, body(): pl.pallas_call(functools.partial(refresh_kernel, n_row=n_row, n_col=n_col...  143 us
    all_gather x1, waiting for transfers between devices, body(): row_g = lax.all_gather(piece, 'col', axis=0, tiled=False)  135 us
    pallas_call x1, Pallas kernels, body(): pl.pallas_call(functools.partial(update_kernel, n_row=n_row, n_col=n_col)...  123 us
    reshape x2, local copies, waits for them, and re-layouts, body(): row_g = row_g.reshape(n_row, ratio, s_local, blocks_b, width)  47.8 us
    another operation x6, other arithmetic, body(): factor = jnp.linalg.cholesky(diag_tile)  34 us
    reshape x1, local copies, waits for them, and re-layouts, body(): jnp.transpose(row_g, (3, 1, 4, 0, 2)).reshape(blocks_a, width, samples)  25.9 us
  transfers between devices with their start and end apart: 6, of which 5 were waited for; matrix products, arithmetic and copies ran while one was open for 1% of the time, Pallas kernels for 0%

profile of v1, /device:TPU:0, one launch (start us, length us, event | category | flops | bytes accessed | tf_op | source)
XLA Modules:
  0.0 907.8 jit_solution(11913947946512783864)
XLA Ops:
  6.5 0.8 convert.5
  7.4 2.9 copy.16
  10.3 1.7 bitcast_multiply_fusion
  12.1 2.2 collective-permute-start
  14.3 1.4 copy-done.1
  16.6 158.2 %all-gather.4.cloned.1.call-done = bf16[1536,10,256]{0,2,1:T(8,128)(2,1)} async-done(((bf16[384,10,256]{0,2,1:T(8,128)(2,1)}), bf16[1536,10,256]{0,2,1:T(8,128)(2,1)}) %all-gather.4.cloned.1.call-update) | async-done | bytes 7864336 | tf_op jit(solution)/shard_map/all_gather | solution.py:85
  174.8 10.4 %copy.18.col_ref = bf16[1536,2560]{1,0:T(8,128)(2,1)} copy(bf16[1536,2560]{0,1:T(8,128)(2,1)} %bitcast.70) | data formatting | bytes 15728640 | tf_op jit(solution)/shard_map/reshape | solution.py:96
  185.2 135.3 %all-gather.6.cloned.1.call-done = bf16[3072,10,256]{0,2,1:T(8,128)(2,1)} async-done(((bf16[384,10,256]{0,2,1:T(8,128)(2,1)}), bf16[3072,10,256]{0,2,1:T(8,128)(2,1)}) %all-gather.6.cloned.1.call-update) | async-done | bytes 15728656 | tf_op jit(solution)/shard_map/all_gather | solution.py:93
  320.5 35.0 %reshape.48 = bf16[4,2,384,10,256]{2,1,0,4,3:T(2,128)(2,1)} reshape(bf16[3072,10,256]{0,2,1:T(8,128)(2,1)} %all-gather.6.cloned.1.call-done) | data formatting | bytes 31457280 | tf_op jit(solution)/shard_map/reshape | solution.py:94
  355.5 12.8 %copy.27 = bf16[4,2,384,10,256]{2,0,4,1,3:T(4,128)(2,1)} copy(bf16[4,2,384,10,256]{2,1,0,4,3:T(2,128)(2,1)} %reshape.48) | data formatting | bytes 31457280 | tf_op jit(solution)/shard_map/reshape | solution.py:94
  368.3 25.9 %reshape.49.rowt_ref = bf16[20,256,1536]{2,1,0:T(8,128)(2,1)} reshape(bf16[10,2,256,4,384]{4,3,2,1,0:T(4,128)(2,1)} %bitcast.69) | data formatting | bytes 31457280 | tf_op jit(solution)/shard_map/reshape | solution.py:95
  394.2 142.8 %shard_map.46.r_ref = f32[20,1,10,1,256,256]{5,4,3,2,1,0:T(8,128)} custom-call(s32[3]{0:T(128)S(1)} %pad_add_fusion.ids_ref, bf16[20,256,1536]{2,1,0:T(8,128)(2,1)} %reshape.49.rowt_ref, bf16[1536,2560]{1,0:T(8,128)(2,1)} %copy.18.col_ref, f32[20,1,10,1,256,256]{5,4,3,2,1,0:T(8,128)} %c_ref.1), custom_call_target="tpu_custom_call" | custom-call | tf_op jit(solution)/shard_map/pallas_call | solution.py:101
  537.0 1.0 constant_dynamic-slice_fusion.1
  538.1 1.0 fusion.7
  539.2 11.7 %cholesky.50 = f32[128,128]{1,0:T(8,128)S(1)} custom-call(f32[128,128]{1,0:T(8,128)S(1)} %cholesky.118), custom_call_target="Cholesky" | custom-call | tf_op jit(solution)/shard_map/jit(cholesky)/cholesky | solution.py:124
  550.9 9.8 %custom-call.14 = f32[1,128,128]{1,2,0:T(8,128)S(1)} custom-call(f32[1,128,128]{2,1,0:T(8,128)S(1)} %get-tuple-element.28), custom_call_target="InvertDiagBlocksLowerTriangular" | custom-call | tf_op jit(solution)/shard_map/jit(cholesky)/cholesky | solution.py:124
  561.2 11.7 %cholesky.105 = f32[128,128]{1,0:T(8,128)S(1)} custom-call(f32[128,128]{1,0:T(8,128)S(1)} %convolution_subtract_fusion.1), custom_call_target="Cholesky" | custom-call | tf_op jit(solution)/shard_map/jit(cholesky)/cholesky | solution.py:124
  573.0 0.7 compare_reduce_fusion
  574.8 0.7 fusion.9
  575.6 3.8 while.1
  575.6 0.6 fusion.24
  576.2 1.3 bitcast_dynamic-update-slice_fusion.2
  577.5 0.6 fusion.24
  578.1 1.3 bitcast_dynamic-update-slice_fusion.2
  579.4 19.9 %custom-call.15 = f32[2,128,128]{1,2,0:T(8,128)S(1)} custom-call(f32[2,128,128]{2,1,0:T(8,128)S(1)} %get-tuple-element.12), custom_call_target="InvertDiagBlocksLowerTriangular" | custom-call | tf_op jit(solution)/shard_map/triangular_solve | solution.py:125
  600.2 0.7 maximum_select_fusion
  601.0 41.2 %all-reduce.5.cloned.1.call-done = f32[256,256]{1,0:T(8,128)} async-done(((f32[256,256]{1,0:T(8,128)}), f32[256,256]{1,0:T(8,128)}) %all-reduce.5.cloned.1.call-update) | async-done | bytes 262160 | tf_op jit(solution)/shard_map/psum | solution.py:15
  642.2 8.3 fusion.3
  650.6 69.2 %all-reduce.7.cloned.1.call-done.prow_ref = bf16[20,256,256]{2,1,0:T(8,128)(2,1)} async-done(((bf16[20,256,256]{2,1,0:T(8,128)(2,1)}), bf16[20,256,256]{2,1,0:T(8,128)(2,1)}) %all-reduce.7.cloned.1.call-update) | async-done | bytes 2621456 | tf_op jit(solution)/shard_map/psum | solution.py:15
  719.8 2.5 fusion.6
  722.3 55.9 %all-reduce.9.cloned.1.call-done.pcol_ref = bf16[10,256,256]{2,1,0:T(8,128)(2,1)} async-done(((bf16[10,256,256]{2,1,0:T(8,128)(2,1)}), bf16[10,256,256]{2,1,0:T(8,128)(2,1)}) %all-reduce.9.cloned.1.call-update) | async-done | bytes 1310736 | tf_op jit(solution)/shard_map/psum | solution.py:15
  778.2 123.0 %shard_map.47 = f32[20,1,10,1,256,256]{5,4,3,2,1,0:T(8,128)} custom-call(s32[3]{0:T(128)} %copy-done, f32[20,1,10,1,256,256]{5,4,3,2,1,0:T(8,128)} %shard_map.46.r_ref, bf16[20,256,256]{2,1,0:T(8,128)(2,1)} %all-reduce.7.cloned.1.call-done.prow_ref, bf16[10,256,256]{2,1,0:T(8,128)(2,1)} %all-reduce.9.cloned.1.call-done.pcol_ref, ...), custom_call_target="tpu_custom_call", output_to_operand_aliasing={{}: (1, {})} | custom-call | tf_op jit(solution)/shard_map/pallas_call | solution.py:145
  (36 shorter events, 2.1 us)
Async XLA Ops:
  6.5 168.3 %all-gather.4.cloned.1.call-start = ((), (), s32[]{:S(2)}) async-start(), calls=%async_computation | async-start | bytes 9830400 | tf_op jit(solution)/shard_map/all_gather | solution.py:85
  12.0 308.5 %all-gather.6.cloned.1.call-start = ((), (), s32[]{:S(2)}) async-start(), calls=%async_computation.4 | async-start | bytes 17694720 | tf_op jit(solution)/shard_map/all_gather | solution.py:93
  12.1 2.2 collective-permute-start
  14.3 1.4 copy-start.1
  15.7 626.6 %all-reduce.5.cloned.1.call-start = ((), (), s32[]{:S(2)}) async-start(), calls=%async_computation.1 | async-start | bytes 524288 | tf_op jit(solution)/shard_map/psum | solution.py:15
  16.5 377.7 %copy-start = (s32[3]{0:T(128)}, s32[3]{0:T(128)S(1)}, u32[]{:S(2)}) copy-start(s32[3]{0:T(128)S(1)} %pad_add_fusion.ids_ref) | copy-start | bytes 40
  600.9 118.9 %all-reduce.7.cloned.1.call-start = ((), (), s32[]{:S(2)}) async-start(), calls=%async_computation.2 | async-start | bytes 5242880 | tf_op jit(solution)/shard_map/psum | solution.py:15
  650.6 127.7 %all-reduce.9.cloned.1.call-start = ((), (), s32[]{:S(2)}) async-start(), calls=%async_computation.3 | async-start | bytes 2621440 | tf_op jit(solution)/shard_map/psum | solution.py:15
Sparse Core Ops, SparseCore 0:
  12.1 162.6 all-gather.3
  176.4 144.0 all-gather.5
  601.0 41.1 all-reduce.4
  650.7 69.1 all-reduce.6
  722.8 55.4 all-reduce.8

commit v2 on v1

v2 whole, which is shorter than its diff:
```python
import functools

import jax
import jax.numpy as jnp
from jax import lax
from jax.experimental import pallas as pl
from jax.experimental.pallas import tpu as pltpu
from jax.sharding import PartitionSpec as P

FORGET = 0.9
NT = (((1,), (1,)), ((), ()))


def from_root(block, axis, holder):
    block = jnp.where(lax.axis_index(axis) == holder, block, jnp.zeros_like(block))
    return lax.psum(block, axis)


def refresh_kernel(ids_ref, row_ref, col_ref, c_ref, o_ref, *, n_row, n_col, blocks_b, samples):
    a = pl.program_id(0)
    r = ids_ref[0]
    c = ids_ref[1]
    i = a * n_row + r
    for b in range(blocks_b):
        j = b * n_col + c

        @pl.when(i >= j)
        def _(b=b):
            acc = None
            for p in range(n_row):
                q = (r - p + n_row) % n_row
                part = lax.dot_general(
                    row_ref[p, 0, 0], col_ref[q, b], NT, preferred_element_type=jnp.float32
                )
                acc = part if acc is None else acc + part
            o_ref[0, 0, b, 0] = FORGET * c_ref[0, 0, b, 0] + acc / samples

        @pl.when(i < j)
        def _(b=b):
            o_ref[0, 0, b, 0] = c_ref[0, 0, b, 0]


def update_kernel(ids_ref, r_ref, prow_ref, pcol_ref, fac_ref, o_ref, *, n_row, n_col, blocks_b):
    a = pl.program_id(0)
    i = a * n_row + ids_ref[0]
    c = ids_ref[1]
    k = ids_ref[2]
    for b in range(blocks_b):
        j = b * n_col + c
        trailing = (i >= j) & (j > k)
        on_column = (j == k) & (i > k)
        on_diagonal = (j == k) & (i == k)
        keep = jnp.logical_not(trailing | on_column | on_diagonal)

        @pl.when(trailing)
        def _(b=b):
            upd = lax.dot_general(prow_ref[0], pcol_ref[b], NT, preferred_element_type=jnp.float32)
            o_ref[0, 0, b, 0] = r_ref[0, 0, b, 0] - upd

        @pl.when(on_column)
        def _(b=b):
            o_ref[0, 0, b, 0] = prow_ref[0].astype(jnp.float32)

        @pl.when(on_diagonal)
        def _(b=b):
            o_ref[0, 0, b, 0] = fac_ref[...]

        @pl.when(keep)
        def _(b=b):
            o_ref[0, 0, b, 0] = r_ref[0, 0, b, 0]


def gather_row(x, n_row):
    parts = [x]
    for s in range(1, n_row):
        parts.append(lax.ppermute(x, "row", [(q, (q + s) % n_row) for q in range(n_row)]))
    return jnp.stack(parts)


def body(covariance, telemetry, active, panel, *, n_row, n_col):
    row_index = lax.axis_index("row")
    col_index = lax.axis_index("col")
    blocks_a = covariance.shape[0]
    blocks_b = covariance.shape[2]
    width = covariance.shape[4]
    ratio = n_col // n_row
    s_local = telemetry.shape[0]
    samples = s_local * n_row
    tiles = blocks_b * n_col
    prior = covariance[:, 0, :, 0]
    mask_full = jnp.concatenate([active, active], axis=1).reshape(tiles, width).astype(jnp.bfloat16)
    col_mask = lax.dynamic_index_in_dim(
        mask_full.reshape(blocks_b, n_col, width), col_index, 1, keepdims=False
    )
    local = telemetry[:, :, 0, :] * col_mask[None]
    local_t = jnp.transpose(local, (1, 2, 0))

    col_t = gather_row(local_t, n_row)
    perm = []
    for src_r in range(n_row):
        for src_c in range(n_col):
            dst_r = src_c % n_row
            dst_c = ratio * src_r + src_c // n_row
            perm.append((src_r * n_col + src_c, dst_r * n_col + dst_c))
    piece = lax.ppermute(local_t, ("row", "col"), perm)
    row_g = lax.all_gather(piece, "col", axis=0, tiled=False)
    row5 = row_g.reshape(n_row, ratio, blocks_b, width, s_local)

    panel_at = panel[0]
    owner_row = panel_at % n_row
    owner_col = panel_at % n_col
    ids = jnp.stack([row_index, col_index, panel_at]).astype(jnp.int32)

    own_diag = lax.dynamic_slice(
        prior, (panel_at // n_row, panel_at // n_col, 0, 0), (1, 1, width, width)
    )[0, 0]
    diag_prior = gather_row(own_diag, n_row)[(row_index - owner_row) % n_row]
    col_k = lax.dynamic_index_in_dim(col_t, panel_at // n_col, 1, keepdims=False)
    gram_kk = jnp.einsum("pts,pus->tu", col_k, col_k, preferred_element_type=jnp.float32)
    diag_tile = FORGET * diag_prior + gram_kk / samples
    factor = jnp.linalg.cholesky(diag_tile)
    inverse = lax.linalg.triangular_solve(
        factor, jnp.eye(width, dtype=jnp.float32), left_side=True, lower=True
    )

    col_k_rp = jnp.take(col_k, (row_index - jnp.arange(n_row)) % n_row, axis=0)
    gram_col = jnp.einsum(
        "phbts,pus->bhtu", row5, col_k_rp, preferred_element_type=jnp.float32
    ).reshape(blocks_a, width, width)
    prior_col = lax.dynamic_index_in_dim(prior, panel_at // n_col, 1, keepdims=False)
    column_part = FORGET * prior_col + gram_col / samples
    row_tiles = jnp.arange(blocks_a, dtype=jnp.int32) * n_row + row_index
    solved = jnp.einsum(
        "atu,vu->atv",
        column_part,
        inverse,
        precision=lax.Precision.HIGHEST,
        preferred_element_type=jnp.float32,
    )
    solved = jnp.where((row_tiles > panel_at)[:, None, None], solved, jnp.zeros_like(solved))
    panel_rows = from_root(solved.astype(jnp.bfloat16), "col", owner_col)
    pick = col_index // n_row
    chosen = lax.dynamic_index_in_dim(
        panel_rows.reshape(blocks_b, ratio, width, width), pick, 1, keepdims=False
    )
    received = None
    for s in range(1, n_row):
        pairs = []
        for cc in range(n_col):
            src_r = cc % n_row
            pairs.append((src_r * n_col + cc, ((src_r + s) % n_row) * n_col + cc))
        got = lax.ppermute(chosen, ("row", "col"), pairs)
        received = got if received is None else received + got
    panel_cols = jnp.where(row_index == col_index % n_row, chosen, received)

    refreshed = pl.pallas_call(
        functools.partial(
            refresh_kernel, n_row=n_row, n_col=n_col, blocks_b=blocks_b, samples=samples
        ),
        out_shape=jax.ShapeDtypeStruct(covariance.shape, jnp.float32),
        grid_spec=pltpu.PrefetchScalarGridSpec(
            num_scalar_prefetch=1,
            grid=(blocks_a,),
            in_specs=[
                pl.BlockSpec(
                    (n_row, 1, 1, width, s_local),
                    lambda a, ids: (0, a % ratio, a // ratio, 0, 0),
                ),
                pl.BlockSpec((n_row, blocks_b, width, s_local), lambda a, ids: (0, 0, 0, 0)),
                pl.BlockSpec(
                    (1, 1, blocks_b, 1, width, width), lambda a, ids: (a, 0, 0, 0, 0, 0)
                ),
            ],
            out_specs=pl.BlockSpec(
                (1, 1, blocks_b, 1, width, width), lambda a, ids: (a, 0, 0, 0, 0, 0)
            ),
        ),
        compiler_params=pltpu.CompilerParams(vmem_limit_bytes=48 * 1024 * 1024),
    )(ids, row5, col_t, covariance)

    result = pl.pallas_call(
        functools.partial(update_kernel, n_row=n_row, n_col=n_col, blocks_b=blocks_b),
        out_shape=jax.ShapeDtypeStruct(covariance.shape, jnp.float32),
        grid_spec=pltpu.PrefetchScalarGridSpec(
            num_scalar_prefetch=1,
            grid=(blocks_a,),
            in_specs=[
                pl.BlockSpec(
                    (1, 1, blocks_b, 1, width, width), lambda a, ids: (a, 0, 0, 0, 0, 0)
                ),
                pl.BlockSpec((1, width, width), lambda a, ids: (a, 0, 0)),
                pl.BlockSpec((blocks_b, width, width), lambda a, ids: (0, 0, 0)),
                pl.BlockSpec((width, width), lambda a, ids: (0, 0)),
            ],
            out_specs=pl.BlockSpec(
                (1, 1, blocks_b, 1, width, width), lambda a, ids: (a, 0, 0, 0, 0, 0)
            ),
        ),
        input_output_aliases={1: 0},
        compiler_params=pltpu.CompilerParams(vmem_limit_bytes=48 * 1024 * 1024),
    )(ids, refreshed, panel_rows, panel_cols, factor)
    return result


def solution(mesh):
    n_row = mesh.shape["row"]
    n_col = mesh.shape["col"]
    in_specs = (P(None, "row", None, "col", None, None), P("row", None, "col", None), P(), P())
    out_specs = P(None, "row", None, "col", None, None)
    return jax.shard_map(
        functools.partial(body, n_row=n_row, n_col=n_col),
        mesh=mesh,
        in_specs=in_specs,
        out_specs=out_specs,
        check_vma=False,
    )
```

time: 917 us -> 543 us (0.59)
  waiting for transfers between devices: 460 us -> 151 us
  Pallas kernels: 266 us -> 112 us
  starting transfers between devices: 2.37 us -> 150 us
  local copies, waits for them, and re-layouts: 93.3 us -> 21.9 us
  matrix products: 9.61 us -> 29 us
    all_gather x1 -> x0, waiting for transfers between devices: 158 us -> none  [body(): column_data = lax.all_gather(local, 'row', axis=0, tiled=True)]
    ppermute x1 -> x10, starting transfers between devices: 2.21 us -> 150 us  [the longest x6 139 us: gather_row(): lax.ppermute(x, 'row', [(q, (q + s) % n_row) for q in range(n_row)])]
    all_gather x1, waiting for transfers between devices: 135 us -> 2.11 us  [body(): row_g = lax.all_gather(piece, 'col', axis=0, tiled=False)]
    reshape x4 -> x0, local copies, waits for them, and re-layouts: 84.1 us -> none  [the longest x2 47.8 us: body(): row_g = row_g.reshape(n_row, ratio, s_local, blocks_b, width)]
    pallas_call x1, Pallas kernels: 123 us -> 42.7 us  [body(): pl.pallas_call(functools.partial(update_kernel, n_row=n_row, n_col=n_col,...]
    psum x3 -> x1, waiting for transfers between devices: 166 us -> 86.8 us  [from_root(): return lax.psum(block, axis)]
    pallas_call x1, Pallas kernels: 143 us -> 69.4 us  [body(): pl.pallas_call(functools.partial(refresh_kernel, n_row=n_row, n_col=n_col...]
    ppermute x1 -> x10, waiting for transfers between devices: 0.01 us -> 62.3 us  [the longest x6 62.3 us: gather_row(): lax.ppermute(x, 'row', [(q, (q + s) % n_row) for q in range(n_row)])]
  transfers between devices with their start and end apart: 6 -> 12, of which waited for: 5 -> 4; matrix products, arithmetic and copies ran while one was open for 1% -> 12% of each run, Pallas kernels for 0% -> 13%
where the time goes in v2:
time: 543 us; the launch traced here: 542 us
  waiting for transfers between devices  151 us (28%)
  starting transfers between devices  150 us (28%)
  Pallas kernels  112 us (21%)
  other arithmetic  62.6 us (12%)
  matrix products  29 us (5%)
  local copies, waits for them, and re-layouts  21.9 us (4%)
  between operations  15.7 us (3%)
    ppermute x6, starting transfers between devices, gather_row(): lax.ppermute(x, 'row', [(q, (q + s) % n_row) for q in range(n_row)])  139 us
    psum x1, waiting for transfers between devices, from_root(): return lax.psum(block, axis)  86.8 us
    pallas_call x1, Pallas kernels, body(): pl.pallas_call(functools.partial(refresh_kernel, n_row=n_row, n_col=n_col...  69.4 us
    ppermute x6, waiting for transfers between devices, gather_row(): lax.ppermute(x, 'row', [(q, (q + s) % n_row) for q in range(n_row)])  62.3 us
    pallas_call x1, Pallas kernels, body(): pl.pallas_call(functools.partial(update_kernel, n_row=n_row, n_col=n_col,...  42.7 us
    another operation x6, other arithmetic, body(): factor = jnp.linalg.cholesky(diag_tile)  34 us
    another operation x3, other arithmetic, body(): lax.linalg.triangular_solve(factor, jnp.eye(width, dtype=jnp.float32), le...  19.9 us
    dot_general x1, matrix products, body(): jnp.einsum('phbts,pus->bhtu', row5, col_k_rp, preferred_element_type=jnp....  17.4 us
  transfers between devices with their start and end apart: 12, of which 4 were waited for; matrix products, arithmetic and copies ran while one was open for 12% of the time, Pallas kernels for 13%

profile of v2, /device:TPU:0, one launch (start us, length us, event | category | flops | bytes accessed | tf_op | source)
XLA Modules:
  0.0 542.1 jit_solution(6212307992407553468)
XLA Ops:
  6.5 0.8 convert.5
  7.4 4.0 copy.31
  11.4 1.9 fusion.10
  13.4 1.3 copy-done.2
  14.7 2.0 collective-permute-start
  16.8 134.5 %collective-permute-start.2 = (bf16[10,256,384]{2,1,0:T(8,128)(2,1)}, bf16[10,256,384]{2,1,0:T(8,128)(2,1)}, u32[]{:S(2)}, u32[]{:S(2)}) collective-permute-start(bf16[10,256,384]{2,1,0:T(8,128)(2,1)} %copy-done.2), channel_id=1, source_target_pairs={{0,16},{8,24},{16,0},{24,8},{1,17},{9,25},{17,1},{25,9},{2,18},{10... | collective-permute-start | bytes 5898248 | tf_op jit(solution)/shard_map/ppermute | solution.py:76
  151.8 2.3 collective-permute-start.3
  154.9 1.0 constant_dynamic-slice_fusion.1
  156.1 1.1 collective-permute-start.5
  157.3 60.0 %collective-permute-done.2 = bf16[10,256,384]{2,1,0:T(8,128)(2,1)} collective-permute-done((bf16[10,256,384]{2,1,0:T(8,128)(2,1)}, bf16[10,256,384]{2,1,0:T(8,128)(2,1)}, u32[]{:S(2)}, u32[]{:S(2)}) %collective-permute-start.2) | collective-permute-done | bytes 1966112 | tf_op jit(solution)/shard_map/ppermute | solution.py:76
  217.3 2.2 collective-permute-done.3
  219.6 3.9 pad_maximum_fusion.col_ref
  223.5 3.1 copy-done.1
  228.1 11.7 %cholesky.50 = f32[128,128]{1,0:T(8,128)S(1)} custom-call(f32[128,128]{1,0:T(8,128)S(1)} %cholesky.118), custom_call_target="Cholesky" | custom-call | tf_op jit(solution)/shard_map/jit(cholesky)/cholesky | solution.py:121
  239.8 9.8 %custom-call.14 = f32[1,128,128]{1,2,0:T(8,128)S(1)} custom-call(f32[1,128,128]{2,1,0:T(8,128)S(1)} %get-tuple-element.30), custom_call_target="InvertDiagBlocksLowerTriangular" | custom-call | tf_op jit(solution)/shard_map/jit(cholesky)/cholesky | solution.py:121
  250.1 11.7 %cholesky.105 = f32[128,128]{1,0:T(8,128)S(1)} custom-call(f32[128,128]{1,0:T(8,128)S(1)} %convolution_subtract_fusion.1), custom_call_target="Cholesky" | custom-call | tf_op jit(solution)/shard_map/jit(cholesky)/cholesky | solution.py:121
  263.9 4.0 while.1
  264.5 1.4 bitcast_dynamic-update-slice_fusion.2
  266.5 1.4 bitcast_dynamic-update-slice_fusion.2
  267.9 19.9 %custom-call.15 = f32[2,128,128]{1,2,0:T(8,128)S(1)} custom-call(f32[2,128,128]{2,1,0:T(8,128)S(1)} %get-tuple-element.12), custom_call_target="InvertDiagBlocksLowerTriangular" | custom-call | tf_op jit(solution)/shard_map/triangular_solve | solution.py:122
  288.6 2.1 all-gather.3.cloned.1.call-done
  290.7 17.4 %fusion = f32[10,2,256,256]{2,3,0,1:T(8,128)} fusion(bf16[4,2,10,256,384]{4,3,2,1,0:T(8,128)(2,1)} %bitcast.125, bf16[4,256,384]{2,1,0:T(8,128)(2,1)S(1)} %gather_fusion, pred[4]{0:T(512)(128)(4,1)S(1)} %compare_and_fusion), kind=kOutput, calls=%fused_computation.5 | convolution fusion | flops 4028235776 | bytes 21757956 | tf_op jit(solution)/shard_map/phbts,pus->bhtu/dot_general | solution.py:127
  308.1 5.9 %copy.34 = f32[10,2,256,256]{3,2,1,0:T(8,128)} copy(f32[10,2,256,256]{2,3,0,1:T(8,128)} %fusion) | data formatting | bytes 10485760 | tf_op jit(solution)/shard_map/div | solution.py:131
  314.0 9.9 %fusion.6 = bf16[20,256,256]{2,1,0:T(8,128)(2,1)} fusion(pred[20]{0:T(512)(128)(4,1)S(1)} %add_compare_fusion, pred[]{:T(512)S(6)} %eq.18, f32[20,256,256]{2,1,0:T(8,128)} %bitcast.124, f32[20,1,10,1,256,256]{5,4,3,2,1,0:T(8,128)} %c_ref.1, s32[]{:T(128)S(6)} %select_n.117, f32[128,256]{1,0:T(8,128)S(1)} %fusion.30, f32[128,256]{1,0:T(8,128)S(1)} %fusion.27), kind=kOutput, calls=%fused_computation.12 | convolution fusion | flops 4033150976 | bytes 13369369 | tf_op jit(solution)/shard_map/atu,vu->atv/dot_general | solution.py:133
  323.9 86.8 %all-reduce.3.cloned.1.call-done.prow_ref = bf16[20,256,256]{2,1,0:T(8,128)(2,1)} async-done(((bf16[20,256,256]{2,1,0:T(8,128)(2,1)}), bf16[20,256,256]{2,1,0:T(8,128)(2,1)}) %all-reduce.3.cloned.1.call-update) | async-done | bytes 2621456 | tf_op jit(solution)/shard_map/psum | solution.py:16
  410.7 1.4 dynamic-slice_bitcast_fusion
  412.1 4.4 collective-permute-start.9
  416.5 2.4 collective-permute-start.8
  418.8 2.4 collective-permute-start.7
  421.3 69.4 %shard_map.46.r_ref = f32[20,1,10,1,256,256]{5,4,3,2,1,0:T(8,128)} custom-call(s32[3]{0:T(128)S(1)} %pad_add_fusion.ids_ref, bf16[4,2,10,256,384]{4,3,2,1,0:T(8,128)(2,1)} %bitcast.126, bf16[4,10,256,384]{3,2,1,0:T(8,128)(2,1)} %copy-done.1, f32[20,1,10,1,256,256]{5,4,3,2,1,0:T(8,128)} %c_ref.1), custom_call_target="tpu_custom_call" | custom-call | tf_op jit(solution)/shard_map/pallas_call | solution.py:156
  490.7 1.9 add_select_fusion.pcol_ref
  492.6 42.7 %shard_map.47 = f32[20,1,10,1,256,256]{5,4,3,2,1,0:T(8,128)} custom-call(s32[3]{0:T(128)S(1)} %pad_add_fusion.ids_ref, f32[20,1,10,1,256,256]{5,4,3,2,1,0:T(8,128)} %shard_map.46.r_ref, bf16[20,256,256]{2,1,0:T(8,128)(2,1)S(1)} %copy-done, bf16[10,256,256]{2,1,0:T(8,128)(2,1)S(1)} %add_select_fusion.pcol_ref, ...), custom_call_target="tpu_custom_call", output_to_operand_aliasing={{}: (1, {})} | custom-call | tf_op jit(solution)/shard_map/pallas_call | solution.py:181
  (53 shorter events, 5.9 us)
Async XLA Ops:
  6.5 284.2 %all-gather.3.cloned.1.call-start = ((), (), s32[]{:S(2)}) async-start(), calls=%async_computation.1 | async-start | bytes 17694720 | tf_op jit(solution)/shard_map/all_gather | solution.py:106
  13.4 1.3 copy-start.2
  14.7 2.0 collective-permute-start
  16.7 394.0 %all-reduce.3.cloned.1.call-start = ((), (), s32[]{:S(2)}) async-start(), calls=%async_computation | async-start | bytes 5242880 | tf_op jit(solution)/shard_map/psum | solution.py:16
  16.8 200.6 %collective-permute-start.2 = (bf16[10,256,384]{2,1,0:T(8,128)(2,1)}, bf16[10,256,384]{2,1,0:T(8,128)(2,1)}, u32[]{:S(2)}, u32[]{:S(2)}) collective-permute-start(bf16[10,256,384]{2,1,0:T(8,128)(2,1)} %copy-done.2), channel_id=1, source_target_pairs={{0,16},{8,24},{16,0},{24,8},{1,17},{9,25},{17,1},{25,9},{2,18},{10... | collective-permute-start | bytes 5898248 | tf_op jit(solution)/shard_map/ppermute | solution.py:76
  151.2 66.1 %collective-permute-start.1 = (bf16[10,256,384]{2,1,0:T(8,128)(2,1)}, bf16[10,256,384]{2,1,0:T(8,128)(2,1)}, u32[]{:S(2)}, u32[]{:S(2)}) collective-permute-start(bf16[10,256,384]{2,1,0:T(8,128)(2,1)} %copy-done.2), channel_id=1, source_target_pairs={{0,8},{8,16},{16,24},{24,0},{1,9},{9,17},{17,25},{25,1},{2,10},{10... | collective-permute-start | bytes 5898248 | tf_op jit(solution)/shard_map/ppermute | solution.py:76
  151.8 67.7 %collective-permute-start.3 = (bf16[10,256,384]{2,1,0:T(8,128)(2,1)}, bf16[10,256,384]{2,1,0:T(8,128)(2,1)}, u32[]{:S(2)}, u32[]{:S(2)}) collective-permute-start(bf16[10,256,384]{2,1,0:T(8,128)(2,1)} %copy-done.2), channel_id=1, source_target_pairs={{0,24},{8,0},{16,8},{24,16},{1,25},{9,1},{17,9},{25,17},{2,26},{10... | collective-permute-start | bytes 5898248 | tf_op jit(solution)/shard_map/ppermute | solution.py:76
  156.0 71.4 %collective-permute-start.6 = (f32[256,256]{0,1:T(8,128)S(1)}, f32[256,256]{0,1:T(8,128)S(1)}, u32[]{:S(2)}, u32[]{:S(2)}) collective-permute-start(f32[256,256]{0,1:T(8,128)S(1)} %bitcast.127), channel_id=1, source_target_pairs={{0,24},{8,0},{16,8},{24,16},{1,25},{9,1},{17,9},{25,17},{2,26},{10... | collective-permute-start | bytes 786440 | tf_op jit(solution)/shard_map/ppermute | solution.py:76
  156.1 71.3 %collective-permute-start.5 = (f32[256,256]{0,1:T(8,128)S(1)}, f32[256,256]{0,1:T(8,128)S(1)}, u32[]{:S(2)}, u32[]{:S(2)}) collective-permute-start(f32[256,256]{0,1:T(8,128)S(1)} %bitcast.128), channel_id=1, source_target_pairs={{0,16},{8,24},{16,0},{24,8},{1,17},{9,25},{17,1},{25,9},{2,18},{10... | collective-permute-start | bytes 786440 | tf_op jit(solution)/shard_map/ppermute | solution.py:76
  217.3 10.1 %collective-permute-start.4 = (f32[256,256]{0,1:T(8,128)S(1)}, f32[256,256]{0,1:T(8,128)S(1)}, u32[]{:S(2)}, u32[]{:S(2)}) collective-permute-start(f32[256,256]{0,1:T(8,128)S(1)} %bitcast.129), channel_id=1, source_target_pairs={{0,8},{8,16},{16,24},{24,0},{1,9},{9,17},{17,25},{25,1},{2,10},{10... | collective-permute-start | bytes 786440 | tf_op jit(solution)/shard_map/ppermute | solution.py:76
  223.5 3.1 copy-start.1
  412.1 78.5 %collective-permute-start.9 = (bf16[10,256,256]{2,1,0:T(8,128)(2,1)S(1)}, bf16[10,256,256]{2,1,0:T(8,128)(2,1)S(1)}, u32[]{:S(2)}, u32[]{:S(2)}) collective-permute-start(bf16[10,256,256]{2,1,0:T(8,128)(2,1)S(1)} %dynamic-slice_bitcast_fusion), channel_id=1, source_target_pairs={{0,24},{9,1},{18,10},{27,19},{4,28},{13,5},{22,14},{31,23}} | collective-permute-start | bytes 3932168 | tf_op jit(solution)/shard_map/ppermute | solution.py:152
  416.5 74.2 %collective-permute-start.8 = (bf16[10,256,256]{2,1,0:T(8,128)(2,1)S(1)}, bf16[10,256,256]{2,1,0:T(8,128)(2,1)}, u32[]{:S(2)}, u32[]{:S(2)}) collective-permute-start(bf16[10,256,256]{2,1,0:T(8,128)(2,1)S(1)} %dynamic-slice_bitcast_fusion), channel_id=1, source_target_pairs={{0,16},{9,25},{18,2},{27,11},{4,20},{13,29},{22,6},{31,15}} | collective-permute-start | bytes 3932168 | tf_op jit(solution)/shard_map/ppermute | solution.py:152
  418.8 71.8 %collective-permute-start.7 = (bf16[10,256,256]{2,1,0:T(8,128)(2,1)S(1)}, bf16[10,256,256]{2,1,0:T(8,128)(2,1)}, u32[]{:S(2)}, u32[]{:S(2)}) collective-permute-start(bf16[10,256,256]{2,1,0:T(8,128)(2,1)S(1)} %dynamic-slice_bitcast_fusion), channel_id=1, source_target_pairs={{0,8},{9,17},{18,26},{27,3},{4,12},{13,21},{22,30},{31,7}} | collective-permute-start | bytes 3932168 | tf_op jit(solution)/shard_map/ppermute | solution.py:152
  421.3 69.4 %copy-start = (bf16[20,256,256]{2,1,0:T(8,128)(2,1)S(1)}, bf16[20,256,256]{2,1,0:T(8,128)(2,1)}, u32[]{:S(2)}) copy-start(bf16[20,256,256]{2,1,0:T(8,128)(2,1)} %all-reduce.3.cloned.1.call-done.prow_ref) | copy-start | bytes 7864324
Sparse Core Ops, SparseCore 0:
  16.8 273.8 all-gather.2
  324.0 86.6 all-reduce.2
